TPU v7x, 32 devices: a whole 2x2x4 slice. The times are simulated.
32 devices in a mesh: groups: 2 (over y), seq: 4 (over x, core), fsdp: 4 (over z).
Axes of the slice: x: 2, y: 2, z: 4, core: 2. Of those that a mesh axis runs over, the one named last changes fastest.
Arguments:
- tokens: bfloat16 [16, 512, 1536], P(('groups', 'fsdp'), 'seq'), parts along dimension 0, may hold values from -6 to 6
- in_weight: bfloat16 [1536, 4608], P(None, 'fsdp'), may hold values from -0.15625 to 0.15625
- short_weight: float32 [3, 4608], replicated, may hold values from -3.5 to 3.5
- basis_in: float32 [17, 64], replicated, may hold values from -4 to 4
- basis_bias: float32 [64], replicated, may hold values from -3.140625 to 3.140625
- basis_mid: float32 [64, 64], replicated, may hold values from -1.5 to 1.5
- basis_shift: float32 [64], replicated, may hold values from -3.140625 to 3.140625
- response_out: float32 [2, 64, 1536], P(None, None, 'fsdp'), may hold values from -0.0234375 to 0.0234375
- skip_gain: float32 [1536], P('fsdp'), may hold values from -4 to 4
- block_counts: int32 [16, 4], P(('groups', 'fsdp'), 'seq'), parts along dimension 0, may hold values from 1 to 128, as said below
Outputs:
- mixed: bfloat16 [16, 512, 1536], P(('groups', 'fsdp'), 'seq'), parts along dimension 0
There are 2 independent parts, one for each index of `groups`. A program takes and returns all parts, laid end to end along the dimension named above; an argument that names none is the same for every part. Nothing has to cross between parts.
Inputs may be any that keep to these rules, and one draw needn't show every extreme that they name: `block_counts`: in every table one block holds all 128 tokens and another holds a single token.
All inputs are finite; a program needn't handle non-finite values.
Results may differ from a plain program's by a relative error of at most 0.007.
Values may be sent and summed in bfloat16 or wider, within the bound.
No kernel may reach another device: no remote copies, remote signals or barrier semaphores. Data moves between devices by JAX's collectives and lax.ppermute only.
A program may use at most 128 MiB of HBM per device.

v0:
```python
import jax
import jax.numpy as jnp
from jax import lax
from jax.sharding import PartitionSpec as P


def padded_2(cells, sides, width):
    for axis, dim in sides:
        count = lax.axis_size(axis)
        ends = count - 1
        head = lax.slice_in_dim(cells, 0, width, axis=dim)
        tail = lax.slice_in_dim(cells, cells.shape[dim] - width, cells.shape[dim], axis=dim)
        cells = jnp.concatenate(
            [
                lax.ppermute(tail, axis, [(i, (i + 1) % count) for i in range(ends)]),
                cells,
                lax.ppermute(head, axis, [((i + 1) % count, i) for i in range(ends)]),
            ],
            axis=dim,
        )
    return cells


def filter_basis(lag_values, total_len, basis_in, basis_bias, basis_mid, basis_shift):
    band_count = (basis_in.shape[0] - 1) // 2
    distance = jnp.abs(lag_values)
    periods = (2 ** (jnp.arange(band_count, dtype=jnp.int32) + 2) + 1).astype(jnp.int32)
    angles = (
        2.0
        * jnp.pi
        * (distance[:, None] % periods[None, :]).astype(jnp.float32)
        / periods[None, :].astype(jnp.float32)
    )
    linear = distance.astype(jnp.float32)[:, None] / total_len
    encoded = jnp.concatenate([linear, jnp.cos(angles), jnp.sin(angles)], axis=1)
    hidden = jnp.sin(jnp.dot(encoded, basis_in, precision=lax.Precision.HIGHEST) + basis_bias)
    return jnp.sin(jnp.dot(hidden, basis_mid, precision=lax.Precision.HIGHEST) + basis_shift)


def forward_table(block_len):
    period = 2 * block_len
    frequency = jnp.arange(block_len, dtype=jnp.int32)[:, None]
    samples = jnp.arange(period, dtype=jnp.int32)[None, :]
    phases = 2.0 * jnp.pi / period * (frequency * samples % period).astype(jnp.float32)
    alternate = (1 - 2 * (samples % 2)).astype(jnp.float32)
    real_rows = jnp.cos(phases)
    imag_rows = jnp.where(frequency == 0, alternate, -jnp.sin(phases))
    return jnp.concatenate([real_rows, imag_rows], axis=0)


def inverse_table(block_len):
    period = 2 * block_len
    places = jnp.arange(block_len, dtype=jnp.int32)[:, None]
    frequency = jnp.arange(block_len, dtype=jnp.int32)[None, :]
    phases = 2.0 * jnp.pi / period * (places * frequency % period).astype(jnp.float32)
    alternate = (1 - 2 * (places % 2)).astype(jnp.float32)
    real_cols = jnp.where(frequency == 0, 1.0, 2.0 * jnp.cos(phases)) / period
    imag_cols = jnp.where(frequency == 0, alternate, -2.0 * jnp.sin(phases)) / period
    return jnp.concatenate([real_cols, imag_cols], axis=1)


def packed_product(response, signal, block_len):
    first_slot = (jnp.arange(block_len) == 0)[:, None]
    resp_real = response[..., :block_len, :]
    resp_imag = response[..., block_len:, :]
    sig_real = signal[..., :block_len, :]
    sig_imag = signal[..., block_len:, :]
    cross_term = resp_imag * sig_imag
    prod_real = resp_real * sig_real - jnp.where(first_slot, 0.0, cross_term)
    prod_imag = jnp.where(first_slot, cross_term, resp_real * sig_imag + resp_imag * sig_real)
    return jnp.concatenate([prod_real, prod_imag], axis=-2)


def shards(
    tokens,
    in_weight,
    short_weight,
    basis_in,
    basis_bias,
    basis_mid,
    basis_shift,
    response_out,
    skip_gain,
    block_counts,
):
    seq_dev, block_len, width = tokens.shape
    group_tokens = lax.all_gather(tokens, "fsdp", axis=0, tiled=True)
    group_rows = group_tokens.shape[0]
    local_cols = in_weight.shape[1]
    partial = jnp.dot(
        group_tokens.reshape(group_rows * block_len, width),
        in_weight,
        preferred_element_type=jnp.float32,
    ).astype(jnp.bfloat16)
    partial = partial.reshape(group_rows, block_len, local_cols)
    projected = lax.all_to_all(partial, "fsdp", 0, 2, tiled=True)
    padded = padded_2(projected, (("seq", 1),), 1)
    shorted = (
        short_weight[0] * padded[:, :-2]
        + short_weight[1] * padded[:, 1:-1]
        + short_weight[2] * padded[:, 2:]
    )
    query_gate = shorted[:, :, :width]
    key_part = shorted[:, :, width : 2 * width]
    value_part = shorted[:, :, 2 * width :]
    valid_mask = (jnp.arange(block_len, dtype=jnp.int32)[None, :] < block_counts).astype(
        jnp.float32
    )
    carried = (key_part * value_part * valid_mask[:, :, None]).astype(jnp.bfloat16)
    local_ch = skip_gain.shape[0]
    params = jnp.concatenate(
        [response_out.reshape(2 * response_out.shape[1], local_ch), skip_gain[None, :]], axis=0
    )
    gathered = lax.all_gather(params, "fsdp", axis=0, tiled=False)
    gathered = jnp.transpose(gathered, (1, 0, 2)).reshape(params.shape[0], width)
    stacked_out = gathered[:-1]
    full_skip = gathered[-1]
    seq_count = lax.axis_size("seq")
    position = lax.axis_index("seq")
    total_len = float(seq_count * block_len)
    forward = forward_table(block_len)
    forward_half = forward[:, :block_len]
    half_hi = forward_half.astype(jnp.bfloat16)
    half_lo = (forward_half - half_hi.astype(jnp.float32)).astype(jnp.bfloat16)
    inverse = inverse_table(block_len)
    circular = jnp.arange(2 * block_len, dtype=jnp.int32)
    wrapped = jnp.where(circular < block_len, circular, circular - 2 * block_len)
    piece = lax.all_gather(carried, "seq", axis=1, tiled=True)
    block_total = piece.shape[1] // block_len
    chunk = min(block_total, 4)

    def chunk_spectrum(first, rows):
        offsets = (position - first - jnp.arange(chunk, dtype=jnp.int32)) * block_len
        lag_values = (offsets[:, None] + wrapped[None, :]).reshape(-1)
        basis_rows = filter_basis(
            lag_values, total_len, basis_in, basis_bias, basis_mid, basis_shift
        )
        ahead_mask = (lag_values >= 0).astype(jnp.float32)[:, None]
        paired = jnp.concatenate([basis_rows * ahead_mask, basis_rows * (1.0 - ahead_mask)], axis=1)
        paired = paired.reshape(chunk, 2 * block_len, paired.shape[-1])
        paired_spec = jnp.einsum("gf,bfk->bgk", forward, paired, precision=lax.Precision.HIGHEST)
        response = jnp.einsum("bgk,kd->bgd", paired_spec, stacked_out, precision=lax.Precision.HIGH)
        blocks = rows.reshape(seq_dev, chunk, block_len, width)
        signal = jnp.einsum(
            "fc,sbcd->sbfd", half_hi, blocks, preferred_element_type=jnp.float32
        ) + jnp.einsum("fc,sbcd->sbfd", half_lo, blocks, preferred_element_type=jnp.float32)
        total = packed_product(response[None, 0], signal[:, 0], block_len)
        for index in range(1, chunk):
            total = total + packed_product(response[None, index], signal[:, index], block_len)
        return total

    if chunk == block_total:
        spectrum = chunk_spectrum(0, piece)
    else:

        def one_chunk(chunk_index, carry):
            rows = lax.dynamic_slice_in_dim(
                piece, chunk_index * chunk * block_len, chunk * block_len, 1
            )
            return carry + chunk_spectrum(chunk_index * chunk, rows)

        spectrum = lax.fori_loop(
            0,
            block_total // chunk,
            one_chunk,
            jnp.zeros((seq_dev, 2 * block_len, width), jnp.float32),
        )
    conv = jnp.einsum("if,sfd->sid", inverse, spectrum, precision=lax.Precision.HIGH)
    return (query_gate * (conv + full_skip * carried.astype(jnp.float32))).astype(jnp.bfloat16)


def solution(mesh):
    placed = (
        P(("groups", "fsdp"), "seq", None),
        P(None, "fsdp"),
        P(),
        P(),
        P(),
        P(),
        P(),
        P(None, None, "fsdp"),
        P("fsdp"),
        P(("groups", "fsdp"), "seq"),
    )
    return jax.shard_map(
        shards,
        mesh=mesh,
        in_specs=placed,
        out_specs=P(("groups", "fsdp"), "seq", None),
        check_vma=False,
    )
```

profile of v0, /device:TPU:0, one launch (start us, length us, event | category | flops | bytes accessed | tf_op | source)
XLA Modules:
  0.0 243.3 jit_solution(17354887653073094636)
XLA Ops:
  6.5 0.7 all-gather.5.cloned.1.call-update
  7.3 67.9 %all-gather.5.cloned.1.call-done = bf16[8,128,1536]{2,1,0:T(8,128)(2,1)} async-done(((bf16[2,128,1536]{2,1,0:T(8,128)(2,1)}), bf16[8,128,1536]{2,1,0:T(8,128)(2,1)}) %all-gather.5.cloned.1.call-update) | async-done | bytes 3145744 | tf_op jit(solution)/shard_map/all_gather | solution.py:87
  75.2 7.5 %convolution_convert_fusion = bf16[1024,1152]{1,0:T(8,128)(2,1)} fusion(bf16[1024,1536]{1,0:T(8,128)(2,1)} %bitcast.106, bf16[1536,1152]{1,0:T(8,128)(2,1)S(1)} %copy-done), kind=kOutput, calls=%fused_computation.2 | convolution fusion | flops 3625058304 | bytes 9043968 | tf_op jit(solution)/shard_map/dot_general | solution.py:90
  82.7 3.8 %all-to-all-start = ((bf16[8,128,1152]{2,1,0:T(8,128)(2,1)}), bf16[8,128,1152]{2,1,0:T(8,128)(2,1)S(1)}, u32[]{:S(2)}, u32[]{:S(2)}) async-start(bf16[8,128,1152]{2,1,0:T(8,128)(2,1)} %bitcast.99), calls=%async_computation | async-start | bytes 4718592 | tf_op jit(solution)/shard_map/all_to_all | solution.py:96
  86.8 53.7 %all-to-all-done = bf16[8,128,1152]{2,1,0:T(8,128)(2,1)S(1)} async-done(((bf16[8,128,1152]{2,1,0:T(8,128)(2,1)}), bf16[8,128,1152]{2,1,0:T(8,128)(2,1)S(1)}, u32[]{:S(2)}, u32[]{:S(2)}) %all-to-all-start) | async-done | bytes 2359328 | tf_op jit(solution)/shard_map/all_to_all | solution.py:96
  140.5 1.4 copy-done.4
  141.9 3.0 %copy.19 = bf16[4,2,128,1152]{2,3,0,1:T(8,128)(2,1)S(1)} copy(bf16[4,2,128,1152]{3,2,1,0:T(8,128)(2,1)} %bitcast.96) | data formatting | bytes 4718592 | tf_op jit(solution)/shard_map/all_to_all | solution.py:96
  145.0 2.9 %fusion.85 = (bf16[2,1,4608]{1,2,0:T(8,128)(2,1)}, bf16[2,1,4608]{1,2,0:T(8,128)(2,1)}) fusion(bf16[2,128,4608]{1,2,0:T(8,128)(2,1)S(1)} %bitcast.92), kind=kLoop, calls=%fused_computation.153 | loop fusion | bytes 73728 | tf_op jit(solution)/shard_map/slice | solution.py:12
  147.9 2.1 copy.22
  150.0 1.3 collective-permute-start.1
  151.3 2.1 copy.20
  153.4 3.0 %collective-permute-start = (bf16[2,1,4608]{2,0,1:T(2,128)(2,1)S(1)}, bf16[2,1,4608]{2,0,1:T(2,128)(2,1)S(1)}, u32[]{:S(2)}, u32[]{:S(2)}) collective-permute-start(bf16[2,1,4608]{2,0,1:T(2,128)(2,1)S(1)} %copy.20), channel_id=1, source_target_pairs={{0,4},{4,8},{8,12},{1,5},{5,9},{9,13},{2,6},{6,10},{10,14},{3,7},{... | collective-permute-start | bytes 55304 | tf_op jit(solution)/shard_map/ppermute | solution.py:15
  156.5 2.0 copy.23
  158.5 2.0 copy.21
  160.4 6.3 %multiply_add_fusion = f32[2,128,4608]{1,2,0:T(8,128)S(1)} fusion(bf16[2,128,4608]{1,2,0:T(8,128)(2,1)S(1)} %bitcast.93, bf16[2,1,4608]{1,2,0:T(8,128)(2,1)} %copy.23, bf16[2,1,4608]{1,2,0:T(8,128)(2,1)} %copy.21, f32[4608]{0:T(1024)S(1)} %get-tuple-element.6, f32[4608]{0:T(1024)S(1)} %get-tuple-element.7, f32[4608]{0:T(1024)S(1)} %get-tuple-element.5), kind=kLoop, calls=%fused_computation.1 | loop fusion | flops 16515072 | bytes 7170048 | tf_op jit(solution)/shard_map/add | solution.py:99
  166.7 2.1 copy-done.2
  168.8 1.0 fusion.22
  170.2 18.9 %all-gather.1 = f32[4,129,384]{2,1,0:T(8,128)S(1)} all-gather(f32[1,129,384]{2,1,0:T(8,128)S(1)} %maximum_bitcast_fusion), channel_id=2, replica_groups=mesh['groups'=2,'seq'=4,'fsdp'=4] {'fsdp'}, dimensions={0}, use_global_device_ids=true | all-gather | bytes 990720 | tf_op jit(solution)/shard_map/all_gather | solution.py:114
  190.8 2.5 %fusion.26 = f32[1024,64]{1,0:T(8,128)S(1)} fusion(f32[17,64]{1,0:T(8,128)S(1)} %copy-done.17, f32[64]{0:T(128)S(1)} %copy-done.20, f32[1024,8]{0,1:T(8,128)S(1)} %get-tuple-element.33, f32[1024,8]{0,1:T(8,128)S(1)} %get-tuple-element.32, f32[1024,1]{0,1:T(1,128)S(1)} %bitcast.104), kind=kOutput, calls=%fused_computation.45 | convolution fusion | flops 13469696 | bytes 336384 | tf_op jit(solution)/shard_map/dot_general | solution.py:36
  193.3 1.5 broadcast_multiply_fusion.1
  194.9 0.9 select_multiply_fusion.1
  196.4 0.7 convolution_bitcast_fusion
  197.1 2.7 %fusion.86 = f32[4,256,1536]{2,1,0:T(8,128)S(1)} fusion(f32[4,256,128]{2,1,0:T(8,128)S(1)} %convolution_bitcast_fusion, f32[128,1536,1]{1,0,2:T(8,128)S(1)} %reshape.231), kind=kOutput, calls=%fused_computation.154 | convolution fusion | flops 1207959552 | bytes 7602176 | tf_op jit(solution)/shard_map/bgk,kd->bgd/dot_general | solution.py:142
  199.7 2.7 %slice_bitcast_fusion.5 = (f32[128,1536]{1,0:T(8,128)}, f32[128,1536]{1,0:T(8,128)}, f32[128,1536]{1,0:T(8,128)}, f32[128,1536]{1,0:T(8,128)}, f32[128,1536]{1,0...) fusion(f32[4,256,1536]{2,1,0:T(8,128)S(1)} %fusion.86), kind=kLoop, calls=%fused_computation.49 | loop fusion | bytes 12582912 | tf_op jit(solution)/shard_map/mul | solution.py:69
  202.5 3.2 %copy.25 = bf16[2,512,1536]{2,1,0:T(8,128)(2,1)S(1)} copy(bf16[2,512,1536]{1,2,0:T(8,128)(2,1)} %all-gather.7.cloned.1.call-done) | data formatting | bytes 6291456 | tf_op jit(solution)/shard_map/all_gather | solution.py:128
  205.7 1.8 fusion.51
  207.4 6.3 %add_bitcast_fusion = f32[2,4,256,1536]{3,2,1,0:T(8,128)} fusion(f32[2,4,1536,256]{2,3,1,0:T(8,128)S(1)} %fusion.51, bf16[2,4,128,1536]{3,2,1,0:T(8,128)(2,1)S(1)} %bitcast.95, f32[128,256]{1,0:T(8,128)S(1)} %get-tuple-element.41, f32[128,256]{1,0:T(8,128)S(1)} %get-tuple-element.40), kind=kOutput, calls=%fused_computation | convolution fusion | flops 808615936 | bytes 28573696 | tf_op jit(solution)/shard_map/fc,sbcd->sbfd/dot_general | solution.py:146
  213.7 8.6 %slice_bitcast_fusion = (f32[2,256,1536]{2,1,0:T(8,128)S(1)}, f32[2,256,1536]{2,1,0:T(8,128)S(1)}, f32[2,256,1536]{2,1,0:T(8,128)}, f32[2,256,1536]{2,1,0:T(8,128)}) fusion(f32[2,4,256,1536]{3,2,1,0:T(8,128)} %add_bitcast_fusion), kind=kLoop, calls=%fused_computation.3 | loop fusion | bytes 25165824 | tf_op jit(solution)/shard_map/squeeze | solution.py:149
  222.3 3.1 %select_subtract_fusion.3 = (f32[2,128,1536]{2,1,0:T(8,128)S(1)}, f32[2,128,1536]{2,1,0:T(8,128)S(1)}) fusion(f32[2,256,1536]{2,1,0:T(8,128)} %get-tuple-element.10, f32[128,1536]{1,0:T(8,128)} %get-tuple-element.18, f32[128,1536]{1,0:T(8,128)} %get-tuple-element.19, pred[128]{0:T(512)(128)(4,1)S(1)} %iota_compare_fusion), kind=kLoop, calls=%fused_computation.38 | loop fusion | flops 3145728 | bytes 7864448 | tf_op jit(solution)/shard_map/sub | solution.py:69
  226.9 1.9 select_subtract_fusion
  228.9 5.3 %fusion.23 = bf16[2,128,1536]{1,2,0:T(8,128)(2,1)} fusion(f32[2,128,4608]{1,2,0:T(8,128)} %copy-done.2, f32[2,128,1536]{2,1,0:T(8,128)S(1)} %get-tuple-element.27, f32[2,128,1536]{2,1,0:T(8,128)S(1)} %get-tuple-element.26, f32[2,128,1536]{2,1,0:T(8,128)S(1)} %get-tuple-element.36, f32[2,128,1536]{2,1,0:T(8,128)S(1)} %get-tuple-element.37, ...), kind=kOutput, calls=%fused_computation.30 | convolution fusion | flops 611483648 | bytes 15865856 | tf_op jit(solution)/shard_map/if,sfd->sid/dot_general | solution.py:168
  234.2 2.3 copy.30
  (74 shorter events, 4.2 us)
Async XLA Ops:
  6.5 68.6 %copy-start = (bf16[1536,1152]{1,0:T(8,128)(2,1)S(1)}, bf16[1536,1152]{1,0:T(8,128)(2,1)}, u32[]{:S(2)}) copy-start(bf16[1536,1152]{1,0:T(8,128)(2,1)} %param.11) | copy-start | bytes 10616836
  6.5 68.6 %all-gather.5.cloned.1.call-start = ((), (), s32[]{:S(2)}) async-start(), calls=%async_computation.1 | async-start | bytes 3932160 | tf_op jit(solution)/shard_map/all_gather | solution.py:87
  82.7 3.8 %copy-start.15 = (f32[3,4608]{1,0:T(4,128)S(1)}, f32[3,4608]{1,0:T(4,128)}, u32[]{:S(2)}) copy-start(f32[3,4608]{1,0:T(4,128)} %param.12) | copy-start | bytes 165892
  82.7 4.0 %copy-start.21 = (s32[2,1]{0,1:T(1,128)S(1)}, s32[2,1]{0,1:T(1,128)}, u32[]{:S(2)}) copy-start(s32[2,1]{0,1:T(1,128)} %param.19) | copy-start | bytes 28
  82.7 57.8 %all-to-all-start = ((bf16[8,128,1152]{2,1,0:T(8,128)(2,1)}), bf16[8,128,1152]{2,1,0:T(8,128)(2,1)S(1)}, u32[]{:S(2)}, u32[]{:S(2)}) async-start(bf16[8,128,1152]{2,1,0:T(8,128)(2,1)} %bitcast.99), calls=%async_computation | async-start | bytes 4718592 | tf_op jit(solution)/shard_map/all_to_all | solution.py:96
  86.5 116.0 %all-gather.7.cloned.1.call-start = ((), (), s32[]{:S(2)}) async-start(), calls=%async_computation.2 | async-start | bytes 3932160 | tf_op jit(solution)/shard_map/all_gather | solution.py:128
  140.5 1.4 copy-start.4
  150.0 6.5 %collective-permute-start.1 = (bf16[2,1,4608]{2,0,1:T(2,128)(2,1)S(1)}, bf16[2,1,4608]{2,0,1:T(2,128)(2,1)S(1)}, u32[]{:S(2)}, u32[]{:S(2)}) collective-permute-start(bf16[2,1,4608]{2,0,1:T(2,128)(2,1)S(1)} %copy.22), channel_id=1, source_target_pairs={{4,0},{8,4},{12,8},{5,1},{9,5},{13,9},{6,2},{10,6},{14,10},{7,3},{... | collective-permute-start | bytes 55304 | tf_op jit(solution)/shard_map/ppermute | solution.py:17
  153.4 5.0 %collective-permute-start = (bf16[2,1,4608]{2,0,1:T(2,128)(2,1)S(1)}, bf16[2,1,4608]{2,0,1:T(2,128)(2,1)S(1)}, u32[]{:S(2)}, u32[]{:S(2)}) collective-permute-start(bf16[2,1,4608]{2,0,1:T(2,128)(2,1)S(1)} %copy.20), channel_id=1, source_target_pairs={{0,4},{4,8},{8,12},{1,5},{5,9},{9,13},{2,6},{6,10},{10,14},{3,7},{... | collective-permute-start | bytes 55304 | tf_op jit(solution)/shard_map/ppermute | solution.py:15
  166.7 2.1 copy-start.2
  168.8 1.3 copy-start.18
  168.8 1.3 copy-start.14
  189.1 1.6 copy-start.17
  189.1 1.6 copy-start.20
  189.1 4.1 %copy-start.16 = (f32[64,64]{1,0:T(8,128)S(1)}, f32[64,64]{1,0:T(8,128)}, u32[]{:S(2)}) copy-start(f32[64,64]{1,0:T(8,128)} %param.15) | copy-start | bytes 49156
  189.2 4.1 %copy-start.19 = (f32[64]{0:T(128)S(1)}, f32[64]{0:T(128)}, u32[]{:S(2)}) copy-start(f32[64]{0:T(128)} %param.16) | copy-start | bytes 772
  222.3 3.3 %copy-start.3 = (f32[2,256,1536]{2,1,0:T(8,128)S(1)}, f32[2,256,1536]{2,1,0:T(8,128)}, u32[]{:S(2)}) copy-start(f32[2,256,1536]{2,1,0:T(8,128)} %get-tuple-element.11) | copy-start | bytes 9437188
  222.3 3.5 %copy-start.6 = (f32[128,1536]{1,0:T(8,128)S(1)}, f32[128,1536]{1,0:T(8,128)}, u32[]{:S(2)}) copy-start(f32[128,1536]{1,0:T(8,128)} %get-tuple-element.12) | copy-start | bytes 2359300
  222.3 3.7 %copy-start.7 = (f32[128,1536]{1,0:T(8,128)S(1)}, f32[128,1536]{1,0:T(8,128)}, u32[]{:S(2)}) copy-start(f32[128,1536]{1,0:T(8,128)} %get-tuple-element.13) | copy-start | bytes 2359300
  222.3 4.0 %copy-start.8 = (f32[128,1536]{1,0:T(8,128)S(1)}, f32[128,1536]{1,0:T(8,128)}, u32[]{:S(2)}) copy-start(f32[128,1536]{1,0:T(8,128)} %get-tuple-element.14) | copy-start | bytes 2359300
  222.3 4.2 %copy-start.9 = (f32[128,1536]{1,0:T(8,128)S(1)}, f32[128,1536]{1,0:T(8,128)}, u32[]{:S(2)}) copy-start(f32[128,1536]{1,0:T(8,128)} %get-tuple-element.15) | copy-start | bytes 2359300
  222.3 4.4 %copy-start.10 = (f32[128,1536]{1,0:T(8,128)S(1)}, f32[128,1536]{1,0:T(8,128)}, u32[]{:S(2)}) copy-start(f32[128,1536]{1,0:T(8,128)} %get-tuple-element.16) | copy-start | bytes 2359300
  222.3 4.6 %copy-start.11 = (f32[128,1536]{1,0:T(8,128)S(1)}, f32[128,1536]{1,0:T(8,128)}, u32[]{:S(2)}) copy-start(f32[128,1536]{1,0:T(8,128)} %get-tuple-element.17) | copy-start | bytes 2359300
  226.9 1.9 copy-start.5
  226.9 1.9 copy-start.12
  226.9 1.9 copy-start.13
  228.9 7.6 %copy-start.1 = (bf16[1536,1152]{1,0:T(8,128)(2,1)S(1)}, bf16[1536,1152]{1,0:T(8,128)(2,1)}, u32[]{:S(2)}) copy-start(bf16[1536,1152]{1,0:T(8,128)(2,1)} %param.11) | copy-start | bytes 10616836
Sparse Core Ops, SparseCore 0:
  8.9 66.1 all-gather.4
  170.0 28.6 all-gather.6
where the time goes:
time: 244 us; the launch traced here: 243 us
  waiting for transfers between devices  122 us (50%)
  local copies, waits for them, and re-layouts  37 us (15%)
  matrix products  28.2 us (12%)
  blocking collectives  18.9 us (8%)
  other arithmetic  14.8 us (6%)
  between operations  13.8 us (6%)
  starting transfers between devices  8.13 us (3%)
    all_gather x1, waiting for transfers between devices, shards(): group_tokens = lax.all_gather(tokens, 'fsdp', axis=0, tiled=True)  67.9 us
    all_to_all x1, waiting for transfers between devices, shards(): projected = lax.all_to_all(partial, 'fsdp', 0, 2, tiled=True)  53.7 us
    all_gather x1, blocking collectives, shards(): gathered = lax.all_gather(params, 'fsdp', axis=0, tiled=False)  18.9 us
    squeeze x1, local copies, waits for them, and re-layouts, chunk_spectrum(): signal[:, index]  8.56 us
    dot_general x1, matrix products, shards(): jnp.dot(group_tokens.reshape(group_rows * block_len, width), in_weight, p...  7.53 us
    dot_general x1, matrix products, chunk_spectrum(): jnp.einsum('fc,sbcd->sbfd', half_lo, blocks, preferred_element_type=jnp.f...  6.29 us
    add x1, other arithmetic, shards(): short_weight[0] * padded[:, :-2] + short_weight[1] * padded[:, 1:-1]  6.29 us
    dot_general x1, matrix products, shards(): jnp.einsum('if,sfd->sid', inverse, spectrum, precision=lax.Precision.HIGH)  5.28 us
  transfers between devices with their start and end apart: 5, of which 2 were waited for; matrix products, arithmetic and copies ran while one was open for 7% of the time, Pallas kernels for 0%

commit v1 on v0

--- a/solution.py
+++ b/solution.py
@@ -84,7 +84,21 @@
     block_counts,
 ):
     seq_dev, block_len, width = tokens.shape
-    group_tokens = lax.all_gather(tokens, "fsdp", axis=0, tiled=True)
+    num_devices = lax.axis_size("fsdp")
+    pages = tuple(((it, (it + 1) % num_devices) for it in range(num_devices)))
+    all_blocks = tuple(((it, (it - 1) % num_devices) for it in range(num_devices)))
+    arr_now, newest = ([tokens], [tokens])
+    for _ in range(num_devices // 2):
+        arr_now.append(lax.ppermute(arr_now[-1], axis_name="fsdp", perm=pages))
+    no = 0
+    while no < (num_devices - 1) // 2:
+        newest.append(lax.ppermute(newest[-1], perm=all_blocks, axis_name="fsdp"))
+        no += 1
+    group_tokens = jnp.roll(
+        jnp.concatenate([*arr_now[::-1], *newest[1:]], axis=0),
+        (lax.axis_index("fsdp") - num_devices // 2) * tokens.shape[0],
+        0,
+    )
     group_rows = group_tokens.shape[0]
     local_cols = in_weight.shape[1]
     partial = jnp.dot(

time: 244 us -> 236 us (0.967)
  waiting for transfers between devices: 122 us -> 102 us
  local copies, waits for them, and re-layouts: 37 us -> 44.4 us
  starting transfers between devices: 8.13 us -> 15 us
    all_gather x1 -> x0, waiting for transfers between devices: 67.9 us -> none  [shards(): group_tokens = lax.all_gather(tokens, 'fsdp', axis=0, tiled=True)]
    ppermute x0 -> x3, waiting for transfers between devices: none -> 49.5 us  [the longest x2 38.6 us: shards(): arr_now.append(lax.ppermute(arr_now[-1], axis_name='fsdp', perm=pages))]
    ppermute x0 -> x3, starting transfers between devices: none -> 6.85 us  [the longest x1 3.82 us: shards(): newest.append(lax.ppermute(newest[-1], perm=all_blocks, axis_name='fsdp'))]
    unnamed x47 -> x56, local copies, waits for them, and re-layouts: 5.05 us -> 11.1 us
  transfers between devices with their start and end apart: 5 -> 7, of which waited for: 2 -> 4; matrix products, arithmetic and copies ran while one was open for 7% -> 9% of each run, Pallas kernels for 0% -> 0%
where the time goes in v1:
time: 236 us; the launch traced here: 235 us
  waiting for transfers between devices  102 us (43%)
  local copies, waits for them, and re-layouts  44.4 us (19%)
  matrix products  26.2 us (11%)
  blocking collectives  19 us (8%)
  starting transfers between devices  15 us (6%)
  other arithmetic  14.8 us (6%)
  between operations  13.8 us (6%)
    all_to_all x1, waiting for transfers between devices, shards(): projected = lax.all_to_all(partial, 'fsdp', 0, 2, tiled=True)  52.3 us
    ppermute x2, waiting for transfers between devices, shards(): arr_now.append(lax.ppermute(arr_now[-1], axis_name='fsdp', perm=pages))  38.6 us
    all_gather x1, blocking collectives, shards(): gathered = lax.all_gather(params, 'fsdp', axis=0, tiled=False)  19 us
    unnamed x56, local copies, waits for them, and re-layouts  11.1 us
    ppermute x1, waiting for transfers between devices, shards(): newest.append(lax.ppermute(newest[-1], perm=all_blocks, axis_name='fsdp'))  10.8 us
    squeeze x1, local copies, waits for them, and re-layouts, chunk_spectrum(): signal[:, index]  8.55 us
    dot_general x1, matrix products, chunk_spectrum(): jnp.einsum('fc,sbcd->sbfd', half_lo, blocks, preferred_element_type=jnp.f...  6.3 us
    add x1, other arithmetic, shards(): short_weight[0] * padded[:, :-2] + short_weight[1] * padded[:, 1:-1]  6.29 us
  transfers between devices with their start and end apart: 7, of which 4 were waited for; matrix products, arithmetic and copies ran while one was open for 9% of the time, Pallas kernels for 0%

profile of v1, /device:TPU:0, one launch (start us, length us, event | category | flops | bytes accessed | tf_op | source)
XLA Modules:
  0.0 235.1 jit_solution(8565896136678591522)
XLA Ops:
  6.5 3.0 %collective-permute-start = (bf16[2,128,1536]{2,1,0:T(8,128)(2,1)}, bf16[2,128,1536]{2,1,0:T(8,128)(2,1)}, u32[]{:S(2)}, u32[]{:S(2)}) collective-permute-start(bf16[2,128,1536]{2,1,0:T(8,128)(2,1)} %param.10), channel_id=1, source_target_pairs={{0,1},{1,2},{2,3},{3,0},{4,5},{5,6},{6,7},{7,4},{8,9},{9,10},{10,1... | collective-permute-start | bytes 2359304 | tf_op jit(solution)/shard_map/ppermute | solution.py:92
  9.6 19.9 %collective-permute-done = bf16[2,128,1536]{2,1,0:T(8,128)(2,1)} collective-permute-done((bf16[2,128,1536]{2,1,0:T(8,128)(2,1)}, bf16[2,128,1536]{2,1,0:T(8,128)(2,1)}, u32[]{:S(2)}, u32[]{:S(2)}) %collective-permute-start) | collective-permute-done | bytes 786464 | tf_op jit(solution)/shard_map/ppermute | solution.py:92
  29.4 3.8 %collective-permute-start.2 = (bf16[2,128,1536]{2,1,0:T(8,128)(2,1)}, bf16[2,128,1536]{2,1,0:T(8,128)(2,1)}, u32[]{:S(2)}, u32[]{:S(2)}) collective-permute-start(bf16[2,128,1536]{2,1,0:T(8,128)(2,1)} %param.10), channel_id=1, source_target_pairs={{0,3},{1,0},{2,1},{3,2},{4,7},{5,4},{6,5},{7,6},{8,11},{9,8},{10,9... | collective-permute-start | bytes 2359304 | tf_op jit(solution)/shard_map/ppermute | solution.py:95
  33.3 18.8 %collective-permute-done.1 = bf16[2,128,1536]{2,1,0:T(8,128)(2,1)} collective-permute-done((bf16[2,128,1536]{2,1,0:T(8,128)(2,1)}, bf16[2,128,1536]{2,1,0:T(8,128)(2,1)}, u32[]{:S(2)}, u32[]{:S(2)}) %collective-permute-start.1) | collective-permute-done | bytes 786464 | tf_op jit(solution)/shard_map/ppermute | solution.py:92
  54.5 10.8 %collective-permute-done.2 = bf16[2,128,1536]{2,1,0:T(8,128)(2,1)} collective-permute-done((bf16[2,128,1536]{2,1,0:T(8,128)(2,1)}, bf16[2,128,1536]{2,1,0:T(8,128)(2,1)}, u32[]{:S(2)}, u32[]{:S(2)}) %collective-permute-start.2) | collective-permute-done | bytes 786464 | tf_op jit(solution)/shard_map/ppermute | solution.py:95
  70.4 5.5 %convolution_convert_fusion = bf16[1024,1152]{1,0:T(8,128)(2,1)} fusion(bf16[1024,1536]{1,0:T(8,128)(2,1)S(1)} %bitcast.99, bf16[1536,1152]{1,0:T(8,128)(2,1)S(1)} %copy-done), kind=kOutput, calls=%fused_computation.2 | convolution fusion | flops 3625058304 | bytes 9043968 | tf_op jit(solution)/shard_map/dot_general | solution.py:104
  75.9 3.8 %all-to-all-start = ((bf16[8,128,1152]{2,1,0:T(8,128)(2,1)}), bf16[8,128,1152]{2,1,0:T(8,128)(2,1)S(1)}, u32[]{:S(2)}, u32[]{:S(2)}) async-start(bf16[8,128,1152]{2,1,0:T(8,128)(2,1)} %bitcast.100), calls=%async_computation | async-start | bytes 4718592 | tf_op jit(solution)/shard_map/all_to_all | solution.py:110
  79.9 52.3 %all-to-all-done = bf16[8,128,1152]{2,1,0:T(8,128)(2,1)S(1)} async-done(((bf16[8,128,1152]{2,1,0:T(8,128)(2,1)}), bf16[8,128,1152]{2,1,0:T(8,128)(2,1)S(1)}, u32[]{:S(2)}, u32[]{:S(2)}) %all-to-all-start) | async-done | bytes 2359328 | tf_op jit(solution)/shard_map/all_to_all | solution.py:110
  132.2 1.4 copy-done.4
  133.6 3.0 %copy.19 = bf16[4,2,128,1152]{2,3,0,1:T(8,128)(2,1)S(1)} copy(bf16[4,2,128,1152]{3,2,1,0:T(8,128)(2,1)} %bitcast.96) | data formatting | bytes 4718592 | tf_op jit(solution)/shard_map/all_to_all | solution.py:110
  136.7 2.9 %fusion.85 = (bf16[2,1,4608]{1,2,0:T(8,128)(2,1)}, bf16[2,1,4608]{1,2,0:T(8,128)(2,1)}) fusion(bf16[2,128,4608]{1,2,0:T(8,128)(2,1)S(1)} %bitcast.92), kind=kLoop, calls=%fused_computation.162 | loop fusion | bytes 73728 | tf_op jit(solution)/shard_map/slice | solution.py:12
  139.6 2.1 copy.22
  141.7 1.3 collective-permute-start.4
  143.0 2.1 copy.20
  145.1 3.0 %collective-permute-start.3 = (bf16[2,1,4608]{2,0,1:T(2,128)(2,1)S(1)}, bf16[2,1,4608]{2,0,1:T(2,128)(2,1)S(1)}, u32[]{:S(2)}, u32[]{:S(2)}) collective-permute-start(bf16[2,1,4608]{2,0,1:T(2,128)(2,1)S(1)} %copy.20), channel_id=1, source_target_pairs={{0,4},{4,8},{8,12},{1,5},{5,9},{9,13},{2,6},{6,10},{10,14},{3,7},{... | collective-permute-start | bytes 55304 | tf_op jit(solution)/shard_map/ppermute | solution.py:15
  148.2 2.0 copy.23
  150.2 2.0 copy.21
  152.1 6.3 %multiply_add_fusion = f32[2,128,4608]{1,2,0:T(8,128)S(1)} fusion(bf16[2,128,4608]{1,2,0:T(8,128)(2,1)S(1)} %bitcast.93, bf16[2,1,4608]{1,2,0:T(8,128)(2,1)} %copy.23, bf16[2,1,4608]{1,2,0:T(8,128)(2,1)} %copy.21, f32[4608]{0:T(1024)S(1)} %get-tuple-element.6, f32[4608]{0:T(1024)S(1)} %get-tuple-element.7, f32[4608]{0:T(1024)S(1)} %get-tuple-element.5), kind=kLoop, calls=%fused_computation.1 | loop fusion | flops 16515072 | bytes 7170048 | tf_op jit(solution)/shard_map/add | solution.py:113
  158.4 2.1 copy-done.2
  161.9 19.0 %all-gather.1 = f32[4,129,384]{2,1,0:T(8,128)S(1)} all-gather(f32[1,129,384]{2,1,0:T(8,128)S(1)} %maximum_bitcast_fusion), channel_id=2, replica_groups=mesh['groups'=2,'seq'=4,'fsdp'=4] {'fsdp'}, dimensions={0}, use_global_device_ids=true | all-gather | bytes 990720 | tf_op jit(solution)/shard_map/all_gather | solution.py:128
  182.6 2.5 %fusion.26 = f32[1024,64]{1,0:T(8,128)S(1)} fusion(f32[17,64]{1,0:T(8,128)S(1)} %copy-done.18, f32[64]{0:T(128)S(1)} %copy-done.21, f32[1024,8]{0,1:T(8,128)S(1)} %get-tuple-element.33, f32[1024,8]{0,1:T(8,128)S(1)} %get-tuple-element.32, f32[1024,1]{0,1:T(1,128)S(1)} %bitcast.105), kind=kOutput, calls=%fused_computation.45 | convolution fusion | flops 13469696 | bytes 336384 | tf_op jit(solution)/shard_map/dot_general | solution.py:36
  185.1 1.5 broadcast_multiply_fusion.1
  188.8 2.7 %fusion.86 = f32[4,256,1536]{2,1,0:T(8,128)S(1)} fusion(f32[4,256,128]{2,1,0:T(8,128)S(1)} %convolution_bitcast_fusion, f32[128,1536,1]{1,0,2:T(8,128)S(1)} %reshape.231), kind=kOutput, calls=%fused_computation.163 | convolution fusion | flops 1207959552 | bytes 7602176 | tf_op jit(solution)/shard_map/bgk,kd->bgd/dot_general | solution.py:156
  191.5 2.7 %slice_bitcast_fusion.5 = (f32[128,1536]{1,0:T(8,128)}, f32[128,1536]{1,0:T(8,128)}, f32[128,1536]{1,0:T(8,128)}, f32[128,1536]{1,0:T(8,128)}, f32[128,1536]{1,0...) fusion(f32[4,256,1536]{2,1,0:T(8,128)S(1)} %fusion.86), kind=kLoop, calls=%fused_computation.49 | loop fusion | bytes 12582912 | tf_op jit(solution)/shard_map/mul | solution.py:69
  194.2 3.2 %copy.25 = bf16[2,512,1536]{2,1,0:T(8,128)(2,1)S(1)} copy(bf16[2,512,1536]{1,2,0:T(8,128)(2,1)} %all-gather.4.cloned.1.call-done) | data formatting | bytes 6291456 | tf_op jit(solution)/shard_map/all_gather | solution.py:142
  197.4 1.8 fusion.51
  199.2 6.3 %add_bitcast_fusion = f32[2,4,256,1536]{3,2,1,0:T(8,128)} fusion(f32[2,4,1536,256]{2,3,1,0:T(8,128)S(1)} %fusion.51, bf16[2,4,128,1536]{3,2,1,0:T(8,128)(2,1)S(1)} %bitcast.95, f32[128,256]{1,0:T(8,128)S(1)} %get-tuple-element.41, f32[128,256]{1,0:T(8,128)S(1)} %get-tuple-element.40), kind=kOutput, calls=%fused_computation | convolution fusion | flops 808615936 | bytes 28573696 | tf_op jit(solution)/shard_map/fc,sbcd->sbfd/dot_general | solution.py:160
  205.5 8.6 %slice_bitcast_fusion = (f32[2,256,1536]{2,1,0:T(8,128)S(1)}, f32[2,256,1536]{2,1,0:T(8,128)S(1)}, f32[2,256,1536]{2,1,0:T(8,128)}, f32[2,256,1536]{2,1,0:T(8,128)}) fusion(f32[2,4,256,1536]{3,2,1,0:T(8,128)} %add_bitcast_fusion), kind=kLoop, calls=%fused_computation.3 | loop fusion | bytes 25165824 | tf_op jit(solution)/shard_map/squeeze | solution.py:163
  214.1 3.1 %select_subtract_fusion.3 = (f32[2,128,1536]{2,1,0:T(8,128)S(1)}, f32[2,128,1536]{2,1,0:T(8,128)S(1)}) fusion(f32[2,256,1536]{2,1,0:T(8,128)} %get-tuple-element.10, f32[128,1536]{1,0:T(8,128)} %get-tuple-element.18, f32[128,1536]{1,0:T(8,128)} %get-tuple-element.19, pred[128]{0:T(512)(128)(4,1)S(1)} %iota_compare_fusion), kind=kLoop, calls=%fused_computation.38 | loop fusion | flops 3145728 | bytes 7864448 | tf_op jit(solution)/shard_map/sub | solution.py:69
  218.7 1.9 select_subtract_fusion
  220.7 5.3 %fusion.23 = bf16[2,128,1536]{1,2,0:T(8,128)(2,1)} fusion(f32[2,128,4608]{1,2,0:T(8,128)} %copy-done.2, f32[2,128,1536]{2,1,0:T(8,128)S(1)} %get-tuple-element.27, f32[2,128,1536]{2,1,0:T(8,128)S(1)} %get-tuple-element.26, f32[2,128,1536]{2,1,0:T(8,128)S(1)} %get-tuple-element.36, f32[2,128,1536]{2,1,0:T(8,128)S(1)} %get-tuple-element.37, ...), kind=kOutput, calls=%fused_computation.30 | convolution fusion | flops 611483648 | bytes 15865856 | tf_op jit(solution)/shard_map/if,sfd->sid/dot_general | solution.py:182
  226.0 2.3 copy.30
  (88 shorter events, 14.2 us)
Async XLA Ops:
  6.5 63.9 %copy-start = (bf16[1536,1152]{1,0:T(8,128)(2,1)S(1)}, bf16[1536,1152]{1,0:T(8,128)(2,1)}, u32[]{:S(2)}) copy-start(bf16[1536,1152]{1,0:T(8,128)(2,1)} %param.11) | copy-start | bytes 10616836
  6.5 22.9 %collective-permute-start = (bf16[2,128,1536]{2,1,0:T(8,128)(2,1)}, bf16[2,128,1536]{2,1,0:T(8,128)(2,1)}, u32[]{:S(2)}, u32[]{:S(2)}) collective-permute-start(bf16[2,128,1536]{2,1,0:T(8,128)(2,1)} %param.10), channel_id=1, source_target_pairs={{0,1},{1,2},{2,3},{3,0},{4,5},{5,6},{6,7},{7,4},{8,9},{9,10},{10,1... | collective-permute-start | bytes 2359304 | tf_op jit(solution)/shard_map/ppermute | solution.py:92
  29.4 22.6 %collective-permute-start.1 = (bf16[2,128,1536]{2,1,0:T(8,128)(2,1)}, bf16[2,128,1536]{2,1,0:T(8,128)(2,1)}, u32[]{:S(2)}, u32[]{:S(2)}) collective-permute-start(bf16[2,128,1536]{2,1,0:T(8,128)(2,1)} %collective-permute-done), channel_id=1, source_target_pairs={{0,1},{1,2},{2,3},{3,0},{4,5},{5,6},{6,7},{7,4},{8,9},{9,10},{10,1... | collective-permute-start | bytes 2359304 | tf_op jit(solution)/shard_map/ppermute | solution.py:92
  29.4 35.9 %collective-permute-start.2 = (bf16[2,128,1536]{2,1,0:T(8,128)(2,1)}, bf16[2,128,1536]{2,1,0:T(8,128)(2,1)}, u32[]{:S(2)}, u32[]{:S(2)}) collective-permute-start(bf16[2,128,1536]{2,1,0:T(8,128)(2,1)} %param.10), channel_id=1, source_target_pairs={{0,3},{1,0},{2,1},{3,2},{4,7},{5,4},{6,5},{7,6},{8,11},{9,8},{10,9... | collective-permute-start | bytes 2359304 | tf_op jit(solution)/shard_map/ppermute | solution.py:95
  33.3 21.2 %copy-start.12 = (bf16[2,128,1536]{2,1,0:T(8,128)(2,1)S(1)}, bf16[2,128,1536]{2,1,0:T(8,128)(2,1)}, u32[]{:S(2)}) copy-start(bf16[2,128,1536]{2,1,0:T(8,128)(2,1)} %param.10) | copy-start | bytes 2359300
  75.8 3.8 %copy-start.16 = (f32[3,4608]{1,0:T(4,128)S(1)}, f32[3,4608]{1,0:T(4,128)}, u32[]{:S(2)}) copy-start(f32[3,4608]{1,0:T(4,128)} %param.12) | copy-start | bytes 165892
  75.9 4.0 %copy-start.22 = (s32[2,1]{0,1:T(1,128)S(1)}, s32[2,1]{0,1:T(1,128)}, u32[]{:S(2)}) copy-start(s32[2,1]{0,1:T(1,128)} %param.19) | copy-start | bytes 28
  75.9 56.4 %all-to-all-start = ((bf16[8,128,1152]{2,1,0:T(8,128)(2,1)}), bf16[8,128,1152]{2,1,0:T(8,128)(2,1)S(1)}, u32[]{:S(2)}, u32[]{:S(2)}) async-start(bf16[8,128,1152]{2,1,0:T(8,128)(2,1)} %bitcast.100), calls=%async_computation | async-start | bytes 4718592 | tf_op jit(solution)/shard_map/all_to_all | solution.py:110
  79.7 114.6 %all-gather.4.cloned.1.call-start = ((), (), s32[]{:S(2)}) async-start(), calls=%async_computation.1 | async-start | bytes 3932160 | tf_op jit(solution)/shard_map/all_gather | solution.py:142
  132.2 1.4 copy-start.4
  141.7 6.5 %collective-permute-start.4 = (bf16[2,1,4608]{2,0,1:T(2,128)(2,1)S(1)}, bf16[2,1,4608]{2,0,1:T(2,128)(2,1)S(1)}, u32[]{:S(2)}, u32[]{:S(2)}) collective-permute-start(bf16[2,1,4608]{2,0,1:T(2,128)(2,1)S(1)} %copy.22), channel_id=1, source_target_pairs={{4,0},{8,4},{12,8},{5,1},{9,5},{13,9},{6,2},{10,6},{14,10},{7,3},{... | collective-permute-start | bytes 55304 | tf_op jit(solution)/shard_map/ppermute | solution.py:17
  145.1 5.0 %collective-permute-start.3 = (bf16[2,1,4608]{2,0,1:T(2,128)(2,1)S(1)}, bf16[2,1,4608]{2,0,1:T(2,128)(2,1)S(1)}, u32[]{:S(2)}, u32[]{:S(2)}) collective-permute-start(bf16[2,1,4608]{2,0,1:T(2,128)(2,1)S(1)} %copy.20), channel_id=1, source_target_pairs={{0,4},{4,8},{8,12},{1,5},{5,9},{9,13},{2,6},{6,10},{10,14},{3,7},{... | collective-permute-start | bytes 55304 | tf_op jit(solution)/shard_map/ppermute | solution.py:15
  158.4 2.1 copy-start.2
  160.5 1.3 copy-start.19
  160.5 1.3 copy-start.15
  180.9 1.6 copy-start.18
  180.9 1.6 copy-start.21
  180.9 4.1 %copy-start.17 = (f32[64,64]{1,0:T(8,128)S(1)}, f32[64,64]{1,0:T(8,128)}, u32[]{:S(2)}) copy-start(f32[64,64]{1,0:T(8,128)} %param.15) | copy-start | bytes 49156
  180.9 4.1 %copy-start.20 = (f32[64]{0:T(128)S(1)}, f32[64]{0:T(128)}, u32[]{:S(2)}) copy-start(f32[64]{0:T(128)} %param.16) | copy-start | bytes 772
  214.1 3.3 %copy-start.3 = (f32[2,256,1536]{2,1,0:T(8,128)S(1)}, f32[2,256,1536]{2,1,0:T(8,128)}, u32[]{:S(2)}) copy-start(f32[2,256,1536]{2,1,0:T(8,128)} %get-tuple-element.11) | copy-start | bytes 9437188
  214.1 3.5 %copy-start.6 = (f32[128,1536]{1,0:T(8,128)S(1)}, f32[128,1536]{1,0:T(8,128)}, u32[]{:S(2)}) copy-start(f32[128,1536]{1,0:T(8,128)} %get-tuple-element.12) | copy-start | bytes 2359300
  214.1 3.7 %copy-start.7 = (f32[128,1536]{1,0:T(8,128)S(1)}, f32[128,1536]{1,0:T(8,128)}, u32[]{:S(2)}) copy-start(f32[128,1536]{1,0:T(8,128)} %get-tuple-element.13) | copy-start | bytes 2359300
  214.1 4.0 %copy-start.8 = (f32[128,1536]{1,0:T(8,128)S(1)}, f32[128,1536]{1,0:T(8,128)}, u32[]{:S(2)}) copy-start(f32[128,1536]{1,0:T(8,128)} %get-tuple-element.14) | copy-start | bytes 2359300
  214.1 4.2 %copy-start.9 = (f32[128,1536]{1,0:T(8,128)S(1)}, f32[128,1536]{1,0:T(8,128)}, u32[]{:S(2)}) copy-start(f32[128,1536]{1,0:T(8,128)} %get-tuple-element.15) | copy-start | bytes 2359300
  214.1 4.4 %copy-start.10 = (f32[128,1536]{1,0:T(8,128)S(1)}, f32[128,1536]{1,0:T(8,128)}, u32[]{:S(2)}) copy-start(f32[128,1536]{1,0:T(8,128)} %get-tuple-element.16) | copy-start | bytes 2359300
  214.1 4.6 %copy-start.11 = (f32[128,1536]{1,0:T(8,128)S(1)}, f32[128,1536]{1,0:T(8,128)}, u32[]{:S(2)}) copy-start(f32[128,1536]{1,0:T(8,128)} %get-tuple-element.17) | copy-start | bytes 2359300
  218.7 1.9 copy-start.5
  218.7 1.9 copy-start.13
  218.7 1.9 copy-start.14
  220.7 7.6 %copy-start.1 = (bf16[1536,1152]{1,0:T(8,128)(2,1)S(1)}, bf16[1536,1152]{1,0:T(8,128)(2,1)}, u32[]{:S(2)}) copy-start(bf16[1536,1152]{1,0:T(8,128)(2,1)} %param.11) | copy-start | bytes 10616836
Sparse Core Ops, SparseCore 0:
  161.7 28.2 all-gather.3
